TPU v7x, 32 devices: a whole 2x2x4 slice. The times are simulated.
32 devices in a mesh: groups: 2 (over y), sec: 4 (over x, core), plane: 4 (over z).
Axes of the slice: x: 2, y: 2, z: 4, core: 2. Of those that a mesh axis runs over, the one named last changes fastest.
Arguments:
- tokens: bfloat16 [16, 512, 1024], P(('groups', 'sec'), 'plane'), parts along dimension 0, may hold values from -8 to 8
- counts: int32 [16], P('groups'), parts along dimension 0, may hold values from 128 to 512, as said below
- region_ids: int32 [16, 512], P(('groups', 'sec'), 'plane'), parts along dimension 0, may hold values from 0 to 31
- norm_gains: float32 [2, 1024], replicated, may hold values from 0.1 to 1.9
- cross_qkv: bfloat16 [1024, 3072], P('plane'), may hold values from -2 to 2
- cross_out: bfloat16 [1024, 1024], P('plane'), may hold values from -0.1875 to 0.1875
- plane_qkv: bfloat16 [1024, 3072], P('plane'), may hold values from -2 to 2
- plane_out: bfloat16 [1024, 1024], P('plane'), may hold values from -0.1875 to 0.1875
Outputs:
- encoded: bfloat16 [16, 512, 1024], P(('groups', 'sec'), 'plane'), parts along dimension 0
- pooled: float32 [64, 1024], P(('groups', 'sec', 'plane')), parts along dimension 0
There are 2 independent parts, one for each index of `groups`. A program takes and returns all parts, laid end to end along the dimension named above; an argument that names none is the same for every part. Nothing has to cross between parts.
Inputs may be any that keep to these rules, and one draw needn't show every extreme that they name: `counts`: valid tissue tokens of each section; they are the first positions of the section.
All inputs are finite; a program needn't handle non-finite values.
Results may differ from a plain program's by a relative error of at most 0.009.
Values may be sent and summed in bfloat16 or wider, within the bound.
No kernel may reach another device: no remote copies, remote signals or barrier semaphores. Data moves between devices by JAX's collectives and lax.ppermute only.
A program may use at most 64 MiB of HBM per device.

v0:
```python
import math
import jax
import jax.numpy as jnp
from jax import lax
from jax.sharding import PartitionSpec as P

HEADS = 16
HEAD_DIM = 64
WINDOW = 128
negative_big = -1e30


def shifted_2(value, axis, by):
    peers = lax.axis_size(axis)
    pairs = [(i, i + by) for i in range(peers) if 0 <= i + by < peers]
    return lax.ppermute(value, axis, pairs)


def rms_norm(values, gain):
    wide = values.astype(jnp.float32)
    scaled = wide * lax.rsqrt(jnp.mean(wide * wide, axis=-1, keepdims=True) + 1e-06) * gain
    return scaled.astype(jnp.bfloat16)


def masked_softmax(scores, allowed):
    shifted = jnp.where(allowed, scores, negative_big)
    top = jnp.max(shifted, axis=-1, keepdims=True)
    expo = jnp.where(allowed, jnp.exp(shifted - top), 0.0)
    return (expo / jnp.sum(expo, axis=-1, keepdims=True)).astype(jnp.bfloat16)


def fold_product(inputs, weight_piece):
    return jnp.dot(inputs, weight_piece, preferred_element_type=jnp.float32)


def gather_pieces(shard):
    groups = lax.axis_size("groups")
    sections = lax.axis_size("sec")
    pair = 2 if sections % 2 == 0 else 1
    width = shard.shape[1] // (groups * pair)
    g = lax.axis_index("groups")
    k = lax.axis_index("sec") % pair
    own = g * pair + k
    mine = lax.dynamic_slice_in_dim(shard, own * width, width, axis=1)
    first = lax.all_gather(mine, "plane", axis=0, tiled=True)
    by_group = [(own, first)]
    for step in range(1, groups):
        moved = [(i, (i + step) % groups) for i in range(groups)]
        source = lax.rem(g - step + groups, groups)
        by_group.append((source * pair + k, lax.ppermute(first, "groups", moved)))
    held = list(by_group)
    if pair == 2:
        swap = [(i, i ^ 1) for i in range(sections)]
        for piece, block in by_group:
            held.append((piece - k + (1 - k), lax.ppermute(block, "sec", swap)))
    return (held, width)


def project(inputs, pieces):
    held, width = pieces
    out = jnp.zeros((inputs.shape[0], width * len(held)), jnp.float32)
    for piece, block in held:
        part = jnp.dot(inputs, block, preferred_element_type=jnp.float32)
        out = lax.dynamic_update_slice_in_dim(out, part, piece * width, axis=1)
    return out


def attend_items(pieces):
    packed_all, flags_all = pieces
    seq_len = packed_all.shape[2]
    block_len = 512
    score_scale = 1.0 / math.sqrt(HEAD_DIM)
    key_index = jnp.arange(seq_len, dtype=jnp.int32)

    def one_item(item_pair):
        packed, key_flag = item_pair
        key_rows = packed[:, HEAD_DIM : 2 * HEAD_DIM]
        value_rows = packed[:, 2 * HEAD_DIM :]
        key_alive = key_flag > 0.5
        query_blocks = packed[:, :HEAD_DIM].reshape(seq_len // block_len, block_len, HEAD_DIM)
        block_starts = jnp.arange(seq_len // block_len, dtype=jnp.int32) * block_len

        def one_block(block_pair):
            query_rows, offset = block_pair
            scores = (
                jnp.einsum("qd,kd->qk", query_rows, key_rows, preferred_element_type=jnp.float32)
                * score_scale
            )
            own_index = offset + jnp.arange(block_len, dtype=jnp.int32)
            allowed = key_alive[None, :] | (key_index[None, :] == own_index[:, None])
            attention = masked_softmax(scores, allowed)
            return jnp.dot(attention, value_rows, preferred_element_type=jnp.float32).astype(
                jnp.bfloat16
            )

        return lax.map(one_block, (query_blocks, block_starts)).reshape(seq_len, HEAD_DIM)

    return lax.map(one_item, (packed_all[0], flags_all[0]))[None]


def body(tokens, counts, region_ids, norm_gains, cross_qkv, cross_out, plane_qkv, plane_out):
    sec_block, tok_block, model_width = tokens.shape
    plane_count = lax.axis_size("plane")
    regions = 2 * lax.axis_size("sec") * plane_count
    positions = lax.axis_index("plane") * tok_block + jnp.arange(tok_block, dtype=jnp.int32)
    padded_counts = jnp.concatenate(
        [jnp.zeros((1,), jnp.int32), counts, jnp.zeros((1,), jnp.int32)]
    )
    near_counts = lax.dynamic_slice_in_dim(
        padded_counts, lax.axis_index("sec") * sec_block, sec_block + 2
    )
    near_valid = positions[None, :] < near_counts[:, None]
    own_valid = near_valid[1 : sec_block + 1]
    score_scale = 1.0 / math.sqrt(HEAD_DIM)
    cross_qkv_pieces = gather_pieces(cross_qkv)
    cross_out_pieces = gather_pieces(cross_out)
    plane_qkv_pieces = gather_pieces(plane_qkv)
    plane_out_pieces = gather_pieces(plane_out)
    normed = rms_norm(tokens, norm_gains[0])
    inputs = normed.reshape(-1, model_width)
    result = project(inputs, cross_qkv_pieces)
    projected = result.astype(jnp.bfloat16).reshape(sec_block, tok_block, 3 * model_width)
    own_kv = projected[:, :, model_width:]
    from_below = shifted_2(own_kv[sec_block - 1], "sec", 1)
    from_above = shifted_2(own_kv[0], "sec", -1)
    near_kv = jnp.concatenate([from_below[None], own_kv, from_above[None]], axis=0)
    queries = projected[:, :, :model_width]
    windows = tok_block // WINDOW
    query_win = queries.reshape(sec_block, windows, WINDOW, HEADS, HEAD_DIM)
    pair_win = near_kv.reshape(sec_block + 2, windows, WINDOW, 2, HEADS, HEAD_DIM)
    stacked = jnp.concatenate(
        [pair_win[0:sec_block], pair_win[1 : sec_block + 1], pair_win[2 : sec_block + 2]], axis=2
    )
    valid_win = near_valid.reshape(sec_block + 2, windows, WINDOW)
    valid_three = jnp.concatenate(
        [valid_win[0:sec_block], valid_win[1 : sec_block + 1], valid_win[2 : sec_block + 2]], axis=2
    )
    itself = jnp.arange(3 * WINDOW)[None, :] == jnp.arange(WINDOW)[:, None] + WINDOW
    scores = (
        jnp.einsum(
            "snqhd,snkhd->snhqk", query_win, stacked[:, :, :, 0], preferred_element_type=jnp.float32
        )
        * score_scale
    )
    allowed = valid_three[:, :, None, None, :] | itself[None, None, None]
    attention = masked_softmax(scores, allowed)
    context = jnp.einsum(
        "snhqk,snkhd->snqhd", attention, stacked[:, :, :, 1], preferred_element_type=jnp.float32
    )
    context = context.astype(jnp.bfloat16).reshape(-1, model_width)
    result = project(context, cross_out_pieces)
    after_cross = (tokens.reshape(-1, model_width).astype(jnp.float32) + result).astype(
        jnp.bfloat16
    )
    normed = rms_norm(after_cross, norm_gains[1])
    result = project(normed, plane_qkv_pieces)
    projected = result.astype(jnp.bfloat16).reshape(sec_block, tok_block, 3, HEADS, HEAD_DIM)
    per_device = sec_block * HEADS // plane_count
    heads_first = jnp.transpose(projected, (0, 3, 1, 2, 4)).reshape(
        plane_count, per_device, tok_block, 3 * HEAD_DIM
    )
    key_flags = jnp.broadcast_to(own_valid[:, None, :], (sec_block, HEADS, tok_block)).astype(
        jnp.bfloat16
    )
    key_flags = key_flags.reshape(plane_count, per_device, tok_block)
    attended = attend_items(
        (
            lax.all_to_all(heads_first, "plane", split_axis=0, concat_axis=2, tiled=True),
            lax.all_to_all(key_flags, "plane", split_axis=0, concat_axis=2, tiled=True),
        )
    )
    returned = lax.all_to_all(attended, "plane", split_axis=2, concat_axis=0, tiled=True)
    context = jnp.transpose(
        returned.reshape(sec_block, HEADS, tok_block, HEAD_DIM), (0, 2, 1, 3)
    ).reshape(-1, model_width)
    result = project(context, plane_out_pieces)
    encoded = (after_cross.astype(jnp.float32) + result).astype(jnp.bfloat16)
    labels = region_ids.reshape(-1)
    member = (jnp.arange(regions, dtype=jnp.int32)[:, None] == labels[None, :]) & own_valid.reshape(
        -1
    )[None, :]
    region_sum = jnp.dot(member.astype(jnp.bfloat16), encoded, preferred_element_type=jnp.float32)
    region_count = jnp.sum(member.astype(jnp.float32), axis=1)
    totals, counted = (
        lax.psum_scatter(region_sum, ("sec", "plane"), scatter_dimension=0, tiled=True),
        lax.psum_scatter(region_count, ("sec", "plane"), scatter_dimension=0, tiled=True),
    )
    pooled = totals / jnp.maximum(counted, 1.0)[:, None]
    return (encoded.reshape(sec_block, tok_block, model_width), pooled)


def solution(mesh):
    in_specs = (
        P(("groups", "sec"), "plane", None),
        P("groups"),
        P(("groups", "sec"), "plane"),
        P(),
        P("plane", None),
        P("plane", None),
        P("plane", None),
        P("plane", None),
    )
    out_specs = (P(("groups", "sec"), "plane", None), P(("groups", "sec", "plane"), None))
    return jax.shard_map(body, mesh=mesh, in_specs=in_specs, out_specs=out_specs, check_vma=False)
```

profile of v0, /device:TPU:8, one launch (start us, length us, event | category | flops | bytes accessed | tf_op | source)
XLA Modules:
  0.0 392.4 jit_solution(481135209715958584)
XLA Ops:
  7.2 1.3 copy-done
  8.6 0.8 constant_dynamic-slice_fusion.3
  9.4 1.8 constant_dynamic-slice_fusion.1
  11.2 35.6 %all-gather.3.cloned.1.call-done = bf16[1024,768]{1,0:T(8,128)(2,1)} async-done(((bf16[256,768]{1,0:T(8,128)(2,1)}), bf16[1024,768]{1,0:T(8,128)(2,1)}) %all-gather.3.cloned.1.call-update) | async-done | bytes 1572880 | tf_op jit(solution)/shard_map/all_gather | solution.py:45
  46.9 1.5 collective-permute-start
  48.3 0.9 constant_dynamic-slice_fusion.2
  49.2 18.7 %all_gather.13 = bf16[1024,256]{1,0:T(8,128)(2,1)} all-gather(bf16[256,256]{1,0:T(8,128)(2,1)S(1)} %constant_dynamic-slice_fusion.2), channel_id=1, replica_groups=mesh['groups'=2,'sec'=4,'plane'=4] {'plane'}, dimensions={0}, use_global_device_ids=true | all-gather | bytes 655360 | tf_op jit(solution)/shard_map/all_gather | solution.py:45
  69.2 15.3 %collective-permute-done = bf16[1024,768]{1,0:T(8,128)(2,1)} collective-permute-done((bf16[1024,768]{1,0:T(8,128)(2,1)}, bf16[1024,768]{1,0:T(8,128)(2,1)}, u32[]{:S(2)}, u32[]{:S(2)}) %collective-permute-start) | collective-permute-done | bytes 1572896 | tf_op jit(solution)/shard_map/ppermute | solution.py:50
  84.7 3.6 all-gather.5.cloned.1.call-done
  88.3 1.4 collective-permute-start.8
  89.8 2.0 convolution_dynamic-update-slice_fusion.7
  91.8 2.0 convolution_dynamic-update-slice_fusion.6
  93.8 2.0 convolution_dynamic-update-slice_fusion.5
  95.8 2.0 convolution_dynamic-update-slice_fusion.4
  97.8 1.1 slice_bitcast_fusion.9
  98.9 2.5 collective-permute-start.3
  101.4 1.5 collective-permute-start.4
  103.1 1.7 collective-permute-start.7
  104.9 0.8 slice.101
  105.7 0.7 copy.52
  106.4 1.3 copy.57
  107.7 20.3 %collective-permute-done.8 = bf16[1024,768]{1,0:T(8,128)(2,1)} collective-permute-done((bf16[1024,768]{1,0:T(8,128)(2,1)}, bf16[1024,768]{1,0:T(8,128)(2,1)}, u32[]{:S(2)}, u32[]{:S(2)}) %collective-permute-start.8) | collective-permute-done | bytes 1572896 | tf_op jit(solution)/shard_map/ppermute | solution.py:50
  128.5 2.7 pad_maximum_fusion.2
  131.3 2.4 copy.53
  133.7 1.3 copy.51
  135.0 2.0 pad_maximum_fusion
  137.0 1.0 fusion.18
  138.0 3.2 fusion.56
  141.3 1.8 fusion.20
  143.8 1.4 convolution_dynamic-update-slice_fusion.15
  145.2 1.4 convolution_dynamic-update-slice_fusion.14
  146.6 1.4 convolution_dynamic-update-slice_fusion.13
  148.0 1.4 convolution_dynamic-update-slice_fusion.12
  149.8 1.2 copy-done.9
  151.6 2.0 convolution_dynamic-update-slice_fusion.2
  153.7 2.0 convolution_dynamic-update-slice_fusion.1
  155.8 2.0 convolution_dynamic-update-slice_fusion
  157.8 0.7 copy.59
  159.3 39.7 %all_to_all.45 = bf16[4,8,128,192]{2,3,1,0:T(8,128)(2,1)S(1)} all-to-all(bf16[4,8,128,192]{2,3,1,0:T(8,128)(2,1)S(1)} %bitcast.141), channel_id=1, replica_groups=mesh['groups'=2,'sec'=4,'plane'=4] {'plane'}, dimensions={0} | all-to-all | bytes 3145728 | tf_op jit(solution)/shard_map/all_to_all | solution.py:168
  199.7 5.0 %all-to-all-start = ((bf16[4,8,128]{2,1,0:T(8,128)(2,1)}), bf16[4,8,128]{2,1,0:T(8,128)(2,1)S(1)}, u32[]{:S(2)}, u32[]{:S(2)}) async-start(bf16[4,8,128]{2,1,0:T(8,128)(2,1)} %broadcast_in_dim.86), calls=%async_computation | async-start | bytes 16384 | tf_op jit(solution)/shard_map/all_to_all | solution.py:169
  204.7 2.6 copy.68
  207.3 1.6 all-to-all-done
  208.9 16.5 %while.11 = (s32[]{:T(128)}, bf16[8,512,64]{1,2,0:T(8,128)(2,1)S(1)}, bf16[8,512]{1,0:T(8,128)(2,1)S(1)}, bf16[8,512,192]{2,1,0:T(8,128)(2,1)}, s32[]{:T(128)}) while((s32[]{:T(128)}, bf16[8,512,64]{1,2,0:T(8,128)(2,1)S(1)}, bf16[8,512]{1,0:T(8,128)(2,1)S(1)}, bf16[8,512,192]{2,1,0:T(8,128)(2,1)}, s32[]{:T(128)}) %tuple.52), condition=%wide.region_7.8_spmd.clone, body=%wide.region_4.7_spmd.clone.sunk | while | flops 71336448 | bytes 3945545 | solution.py:98
  208.9 1.0 dynamic-slice_bitcast_fusion.2
  211.0 1.0 dynamic-slice_bitcast_fusion.2
  213.0 1.0 dynamic-slice_bitcast_fusion.2
  215.1 1.0 dynamic-slice_bitcast_fusion.2
  217.1 1.0 dynamic-slice_bitcast_fusion.2
  219.2 1.0 dynamic-slice_bitcast_fusion.2
  221.3 1.0 dynamic-slice_bitcast_fusion.2
  223.3 1.0 dynamic-slice_bitcast_fusion.2
  225.4 0.8 copy.63
  226.3 1.6 reshape.161
  227.8 4.8 %all-to-all-start.2 = ((bf16[4,2,32768]{2,1,0:T(2,128)(2,1)}), bf16[4,2,32768]{2,1,0:T(2,128)(2,1)S(1)}, u32[]{:S(2)}, u32[]{:S(2)}) async-start(bf16[4,2,32768]{2,1,0:T(2,128)(2,1)} %reshape.161), calls=%async_computation.2 | async-start | bytes 1048576 | tf_op jit(solution)/shard_map/all_to_all | solution.py:172
  232.6 0.9 constant_dynamic-slice_fusion
  233.5 21.6 %all_gather.15 = bf16[1024,256]{1,0:T(8,128)(2,1)S(1)} all-gather(bf16[256,256]{1,0:T(8,128)(2,1)S(1)} %constant_dynamic-slice_fusion), channel_id=1, replica_groups=mesh['groups'=2,'sec'=4,'plane'=4] {'plane'}, dimensions={0}, use_global_device_ids=true | all-gather | bytes 655360 | tf_op jit(solution)/shard_map/all_gather | solution.py:45
  255.2 1.4 collective-permute-start.11
  258.0 30.8 %all-reduce.1 = f32[32]{0:T(128)S(1)} all-reduce(f32[32]{0:T(128)S(1)} %convert_reduce_fusion), channel_id=3, replica_groups=mesh['groups'=2,'sec'=4,'plane'=4] {'sec','plane'}, use_global_device_ids=true, to_apply=%region_10.11.clone | all-reduce | flops 32 | bytes 256
  288.9 0.7 reshape.162
  289.7 0.8 copy.69
  292.0 1.4 convolution_dynamic-update-slice_fusion.9
  294.1 0.8 fusion.43
  295.0 89.5 %all-reduce.4.cloned.1.call-done = f32[32,1024]{1,0:T(8,128)} async-done(((f32[32,1024]{1,0:T(8,128)}), f32[32,1024]{1,0:T(8,128)}) %all-reduce.4.cloned.1.call-update) | async-done | bytes 131088
  384.5 1.4 dynamic-slice_divide_fusion
  (118 shorter events, 17.1 us)
Async XLA Ops:
  7.2 1.4 copy-start
  7.2 39.7 %all-gather.3.cloned.1.call-start = ((), (), s32[]{:S(2)}) async-start(), calls=%async_computation.3 | async-start | bytes 1966080 | tf_op jit(solution)/shard_map/all_gather | solution.py:45
  8.6 59.7 %copy-start.10 = (s32[8]{0:T(128)S(1)}, s32[8]{0:T(128)}, u32[]{:S(2)}) copy-start(s32[8]{0:T(128)} %param.11) | copy-start | bytes 100
  8.6 60.5 %copy-start.2 = (bf16[2,128,1024]{2,1,0:T(8,128)(2,1)S(1)}, bf16[2,128,1024]{2,1,0:T(8,128)(2,1)}, u32[]{:S(2)}) copy-start(bf16[2,128,1024]{2,1,0:T(8,128)(2,1)} %param.10) | copy-start | bytes 1572868
  9.4 75.1 %copy-start.7 = (f32[2,1024]{1,0:T(2,128)S(1)}, f32[2,1024]{1,0:T(2,128)}, u32[]{:S(2)}) copy-start(f32[2,1024]{1,0:T(2,128)} %param.13) | copy-start | bytes 24580
  9.4 78.9 %all-gather.5.cloned.1.call-start = ((), (), s32[]{:S(2)}) async-start(), calls=%async_computation.4 | async-start | bytes 1966080 | tf_op jit(solution)/shard_map/all_gather | solution.py:45
  46.9 37.6 %collective-permute-start = (bf16[1024,768]{1,0:T(8,128)(2,1)}, bf16[1024,768]{1,0:T(8,128)(2,1)}, u32[]{:S(2)}, u32[]{:S(2)}) collective-permute-start(bf16[1024,768]{1,0:T(8,128)(2,1)} %all-gather.3.cloned.1.call-done), channel_id=1, source_target_pairs={{0,16},{16,0},{1,17},{17,1},{2,18},{18,2},{3,19},{19,3},{4,20},{20... | collective-permute-start | bytes 4718600 | tf_op jit(solution)/shard_map/ppermute | solution.py:50
  67.9 35.1 %collective-permute-start.5 = (bf16[1024,256]{1,0:T(8,128)(2,1)}, bf16[1024,256]{1,0:T(8,128)(2,1)}, u32[]{:S(2)}, u32[]{:S(2)}) collective-permute-start(bf16[1024,256]{1,0:T(8,128)(2,1)} %all_gather.13), channel_id=1, source_target_pairs={{0,16},{16,0},{1,17},{17,1},{2,18},{18,2},{3,19},{19,3},{4,20},{20... | collective-permute-start | bytes 1572872 | tf_op jit(solution)/shard_map/ppermute | solution.py:50
  68.3 78.3 %collective-permute-start.6 = (bf16[1024,256]{1,0:T(8,128)(2,1)}, bf16[1024,256]{1,0:T(8,128)(2,1)}, u32[]{:S(2)}, u32[]{:S(2)}) collective-permute-start(bf16[1024,256]{1,0:T(8,128)(2,1)} %all_gather.13), channel_id=1, source_target_pairs={{0,4},{4,0},{8,12},{12,8},{1,5},{5,1},{9,13},{13,9},{2,6},{6,2},{1... | collective-permute-start | bytes 1572872 | tf_op jit(solution)/shard_map/ppermute | solution.py:55
  68.5 25.3 %collective-permute-start.1 = (bf16[1024,768]{1,0:T(8,128)(2,1)}, bf16[1024,768]{1,0:T(8,128)(2,1)}, u32[]{:S(2)}, u32[]{:S(2)}) collective-permute-start(bf16[1024,768]{1,0:T(8,128)(2,1)} %all-gather.3.cloned.1.call-done), channel_id=1, source_target_pairs={{0,4},{4,0},{8,12},{12,8},{1,5},{5,1},{9,13},{13,9},{2,6},{6,2},{1... | collective-permute-start | bytes 4718600 | tf_op jit(solution)/shard_map/ppermute | solution.py:55
  84.5 11.3 %collective-permute-start.2 = (bf16[1024,768]{1,0:T(8,128)(2,1)}, bf16[1024,768]{1,0:T(8,128)(2,1)}, u32[]{:S(2)}, u32[]{:S(2)}) collective-permute-start(bf16[1024,768]{1,0:T(8,128)(2,1)} %collective-permute-done), channel_id=1, source_target_pairs={{0,4},{4,0},{8,12},{12,8},{1,5},{5,1},{9,13},{13,9},{2,6},{6,2},{1... | collective-permute-start | bytes 4718600 | tf_op jit(solution)/shard_map/ppermute | solution.py:55
  88.3 39.8 %collective-permute-start.8 = (bf16[1024,768]{1,0:T(8,128)(2,1)}, bf16[1024,768]{1,0:T(8,128)(2,1)}, u32[]{:S(2)}, u32[]{:S(2)}) collective-permute-start(bf16[1024,768]{1,0:T(8,128)(2,1)} %all-gather.5.cloned.1.call-done), channel_id=1, source_target_pairs={{0,16},{16,0},{1,17},{17,1},{2,18},{18,2},{3,19},{19,3},{4,20},{20... | collective-permute-start | bytes 4718600 | tf_op jit(solution)/shard_map/ppermute | solution.py:50
  98.9 29.1 %collective-permute-start.3 = (bf16[128,2048]{1,0:T(8,128)(2,1)}, bf16[128,2048]{1,0:T(8,128)(2,1)}, u32[]{:S(2)}, u32[]{:S(2)}) collective-permute-start(bf16[128,2048]{1,0:T(8,128)(2,1)} %get-tuple-element.85), channel_id=1, source_target_pairs={{0,4},{4,8},{8,12},{1,5},{5,9},{9,13},{2,6},{6,10},{10,14},{3,7},{... | collective-permute-start | bytes 1572872 | tf_op jit(solution)/shard_map/ppermute | solution.py:16
  101.4 27.1 %collective-permute-start.4 = (bf16[128,2048]{1,0:T(8,128)(2,1)}, bf16[128,2048]{1,0:T(8,128)(2,1)}, u32[]{:S(2)}, u32[]{:S(2)}) collective-permute-start(bf16[128,2048]{1,0:T(8,128)(2,1)} %get-tuple-element.86), channel_id=1, source_target_pairs={{4,0},{8,4},{12,8},{5,1},{9,5},{13,9},{6,2},{10,6},{14,10},{7,3},{... | collective-permute-start | bytes 1572872 | tf_op jit(solution)/shard_map/ppermute | solution.py:16
  103.1 44.9 %collective-permute-start.7 = (bf16[1024,256]{1,0:T(8,128)(2,1)}, bf16[1024,256]{1,0:T(8,128)(2,1)}, u32[]{:S(2)}, u32[]{:S(2)}) collective-permute-start(bf16[1024,256]{1,0:T(8,128)(2,1)} %collective-permute-done.5), channel_id=1, source_target_pairs={{0,4},{4,0},{8,12},{12,8},{1,5},{5,1},{9,13},{13,9},{2,6},{6,2},{1... | collective-permute-start | bytes 1572872 | tf_op jit(solution)/shard_map/ppermute | solution.py:55
  128.0 25.7 %collective-permute-start.9 = (bf16[1024,768]{1,0:T(8,128)(2,1)}, bf16[1024,768]{1,0:T(8,128)(2,1)}, u32[]{:S(2)}, u32[]{:S(2)}) collective-permute-start(bf16[1024,768]{1,0:T(8,128)(2,1)} %all-gather.5.cloned.1.call-done), channel_id=1, source_target_pairs={{0,4},{4,0},{8,12},{12,8},{1,5},{5,1},{9,13},{13,9},{2,6},{6,2},{1... | collective-permute-start | bytes 4718600 | tf_op jit(solution)/shard_map/ppermute | solution.py:55
  128.0 27.7 %collective-permute-start.10 = (bf16[1024,768]{1,0:T(8,128)(2,1)}, bf16[1024,768]{1,0:T(8,128)(2,1)}, u32[]{:S(2)}, u32[]{:S(2)}) collective-permute-start(bf16[1024,768]{1,0:T(8,128)(2,1)} %collective-permute-done.8), channel_id=1, source_target_pairs={{0,4},{4,0},{8,12},{12,8},{1,5},{5,1},{9,13},{13,9},{2,6},{6,2},{1... | collective-permute-start | bytes 4718600 | tf_op jit(solution)/shard_map/ppermute | solution.py:55
  131.3 2.4 copy-start.3
  149.4 1.6 copy-start.9
  149.6 6.1 %copy-start.5 = (bf16[256,1024]{1,0:T(8,128)(2,1)}, bf16[256,1024]{1,0:T(8,128)(2,1)S(1)}, u32[]{:S(2)}) copy-start(bf16[256,1024]{1,0:T(8,128)(2,1)S(1)} %get-tuple-element.82) | copy-start | bytes 1572868
  199.7 9.2 %all-to-all-start = ((bf16[4,8,128]{2,1,0:T(8,128)(2,1)}), bf16[4,8,128]{2,1,0:T(8,128)(2,1)S(1)}, u32[]{:S(2)}, u32[]{:S(2)}) async-start(bf16[4,8,128]{2,1,0:T(8,128)(2,1)} %broadcast_in_dim.86), calls=%async_computation | async-start | bytes 16384 | tf_op jit(solution)/shard_map/all_to_all | solution.py:169
  226.2 30.4 %copy-start.8 = (s32[2,128]{1,0:T(2,128)S(1)}, s32[2,128]{1,0:T(2,128)}, u32[]{:S(2)}) copy-start(s32[2,128]{1,0:T(2,128)} %param.12) | copy-start | bytes 3076
  226.2 30.5 %copy-start.11 = (u32[32]{0:T(128)S(1)}, u32[32]{0:T(128)}, u32[]{:S(2)}) copy-start(u32[32]{0:T(128)} %constant.117) | copy-start | bytes 388
  227.8 61.1 %all-to-all-start.2 = ((bf16[4,2,32768]{2,1,0:T(2,128)(2,1)}), bf16[4,2,32768]{2,1,0:T(2,128)(2,1)S(1)}, u32[]{:S(2)}, u32[]{:S(2)}) async-start(bf16[4,2,32768]{2,1,0:T(2,128)(2,1)} %reshape.161), calls=%async_computation.2 | async-start | bytes 1048576 | tf_op jit(solution)/shard_map/all_to_all | solution.py:172
  232.6 151.8 %all-reduce.4.cloned.1.call-start = ((), (), s32[]{:S(2)}) async-start(), calls=%async_computation.5 | async-start | bytes 262144
  255.2 33.7 %collective-permute-start.11 = (bf16[1024,256]{1,0:T(8,128)(2,1)S(1)}, bf16[1024,256]{1,0:T(8,128)(2,1)S(1)}, u32[]{:S(2)}, u32[]{:S(2)}) collective-permute-start(bf16[1024,256]{1,0:T(8,128)(2,1)S(1)} %all_gather.15), channel_id=1, source_target_pairs={{0,16},{16,0},{1,17},{17,1},{2,18},{18,2},{3,19},{19,3},{4,20},{20... | collective-permute-start | bytes 1572872 | tf_op jit(solution)/shard_map/ppermute | solution.py:50
  256.6 35.4 %collective-permute-start.12 = (bf16[1024,256]{1,0:T(8,128)(2,1)S(1)}, bf16[1024,256]{1,0:T(8,128)(2,1)}, u32[]{:S(2)}, u32[]{:S(2)}) collective-permute-start(bf16[1024,256]{1,0:T(8,128)(2,1)S(1)} %all_gather.15), channel_id=1, source_target_pairs={{0,4},{4,0},{8,12},{12,8},{1,5},{5,1},{9,13},{13,9},{2,6},{6,2},{1... | collective-permute-start | bytes 1572872 | tf_op jit(solution)/shard_map/ppermute | solution.py:55
  288.9 4.7 %collective-permute-start.13 = (bf16[1024,256]{1,0:T(8,128)(2,1)S(1)}, bf16[1024,256]{1,0:T(8,128)(2,1)S(1)}, u32[]{:S(2)}, u32[]{:S(2)}) collective-permute-start(bf16[1024,256]{1,0:T(8,128)(2,1)S(1)} %collective-permute-done.11), channel_id=1, source_target_pairs={{0,4},{4,0},{8,12},{12,8},{1,5},{5,1},{9,13},{13,9},{2,6},{6,2},{1... | collective-permute-start | bytes 1572872 | tf_op jit(solution)/shard_map/ppermute | solution.py:55
  292.0 1.9 copy-start.6
  293.5 92.4 %copy-start.1 = (bf16[256,3072]{1,0:T(8,128)(2,1)S(1)}, bf16[256,3072]{1,0:T(8,128)(2,1)}, u32[]{:S(2)}) copy-start(bf16[256,3072]{1,0:T(8,128)(2,1)} %param.14) | copy-start | bytes 4718596
  294.0 91.9 %copy-start.4 = (bf16[256,1024]{1,0:T(8,128)(2,1)}, bf16[256,1024]{1,0:T(8,128)(2,1)S(1)}, u32[]{:S(2)}) copy-start(bf16[256,1024]{1,0:T(8,128)(2,1)S(1)} %fusion.24) | copy-start | bytes 1572868
Sparse Core Ops, SparseCore 0:
  9.6 37.2 all-gather.2
  49.0 39.2 all-gather.4
  295.0 89.3 all-reduce.3
where the time goes:
time: 394 us; the launch traced here: 392 us
  waiting for transfers between devices  166 us (42%)
  blocking collectives  111 us (28%)
  local copies, waits for them, and re-layouts  33.4 us (8%)
  matrix products  32.7 us (8%)
  starting transfers between devices  21.3 us (5%)
  between operations  15 us (4%)
  other arithmetic  12.9 us (3%)
    unnamed x4, waiting for transfers between devices  89.5 us
    all_gather x2, blocking collectives, gather_pieces(): first = lax.all_gather(mine, 'plane', axis=0, tiled=True)  40.4 us
    all_to_all x1, blocking collectives, body(): lax.all_to_all(heads_first, 'plane', split_axis=0, concat_axis=2, tiled=T...  39.7 us
    all_gather x2, waiting for transfers between devices, gather_pieces(): first = lax.all_gather(mine, 'plane', axis=0, tiled=True)  39.2 us
    ppermute x4, waiting for transfers between devices, gather_pieces(): by_group.append((source * pair + k, lax.ppermute(first, 'groups', moved)))  35.6 us
    unnamed x1, blocking collectives  30.8 us
    dot_general x16, matrix products, project(): part = jnp.dot(inputs, block, preferred_element_type=jnp.float32)  22.8 us
    unnamed x29, local copies, waits for them, and re-layouts  8.08 us
  transfers between devices with their start and end apart: 19, of which 6 were waited for; matrix products, arithmetic and copies ran while one was open for 13% of the time, Pallas kernels for 0%

commit v1 on v0

--- a/solution.py
+++ b/solution.py
@@ -42,7 +42,14 @@
     k = lax.axis_index("sec") % pair
     own = g * pair + k
     mine = lax.dynamic_slice_in_dim(shard, own * width, width, axis=1)
-    first = lax.all_gather(mine, "plane", axis=0, tiled=True)
+    ring = [mine]
+    for hop in range(3):
+        ring.append(lax.ppermute(ring[-1], "plane", [(dev, (dev + 1) % 4) for dev in range(4)]))
+    first = jnp.roll(
+        jnp.concatenate(ring[::-1], axis=0),
+        (lax.axis_index("plane") + 1) * ring[0].shape[0],
+        axis=0,
+    )
     by_group = [(own, first)]
     for step in range(1, groups):
         moved = [(i, (i + step) % groups) for i in range(groups)]

time: 394 us -> 402 us (1.020); the launches traced: 392 us -> 396 us
  blocking collectives: 111 us -> 30.6 us
  waiting for transfers between devices: 166 us -> 199 us
  other arithmetic: 12.9 us -> 42.8 us
  starting transfers between devices: 21.3 us -> 45.8 us
    ppermute x0 -> x12, waiting for transfers between devices: none -> 82.2 us  [gather_pieces(): lax.ppermute(ring[-1], 'plane', [(dev, (dev + 1) % 4) for dev in range(4)])]
    all_gather x2 -> x0, blocking collectives: 40.4 us -> none  [gather_pieces(): first = lax.all_gather(mine, 'plane', axis=0, tiled=True)]
    all_to_all x1 -> x0, blocking collectives: 39.7 us -> none  [body(): lax.all_to_all(heads_first, 'plane', split_axis=0, concat_axis=2, tiled=T...]
    all_gather x2 -> x0, waiting for transfers between devices: 39.2 us -> none  [gather_pieces(): first = lax.all_gather(mine, 'plane', axis=0, tiled=True)]
    concatenate x0 -> x4, other arithmetic: none -> 29 us  [gather_pieces(): jnp.roll(jnp.concatenate(ring[::-1], axis=0), (lax.axis_index('plane') +...]
    ppermute x0 -> x12, starting transfers between devices: none -> 17.2 us  [gather_pieces(): lax.ppermute(ring[-1], 'plane', [(dev, (dev + 1) % 4) for dev in range(4)])]
    ppermute x4, waiting for transfers between devices: 35.6 us -> 26.7 us  [gather_pieces(): by_group.append((source * pair + k, lax.ppermute(first, 'groups', moved)))]
    all_to_all x0 -> x1, starting transfers between devices: none -> 6.91 us  [body(): lax.all_to_all(heads_first, 'plane', split_axis=0, concat_axis=2, tiled=T...]
  transfers between devices with their start and end apart: 19 -> 30, of which waited for: 6 -> 9; matrix products, arithmetic and copies ran while one was open for 13% -> 24% of each run, Pallas kernels for 0% -> 0%
where the time goes in v1:
time: 402 us; the launch traced here: 396 us
  waiting for transfers between devices  199 us (50%)
  starting transfers between devices  45.8 us (11%)
  other arithmetic  42.8 us (11%)
  matrix products  31.4 us (8%)
  local copies, waits for them, and re-layouts  30.6 us (8%)
  blocking collectives  30.6 us (8%)
  between operations  15.5 us (4%)
    unnamed x2, waiting for transfers between devices  90.1 us
    ppermute x12, waiting for transfers between devices, gather_pieces(): lax.ppermute(ring[-1], 'plane', [(dev, (dev + 1) % 4) for dev in range(4)])  82.2 us
    unnamed x1, blocking collectives  30.6 us
    concatenate x4, other arithmetic, gather_pieces(): jnp.roll(jnp.concatenate(ring[::-1], axis=0), (lax.axis_index('plane') +...  29 us
    ppermute x4, waiting for transfers between devices, gather_pieces(): by_group.append((source * pair + k, lax.ppermute(first, 'groups', moved)))  26.7 us
    dot_general x16, matrix products, project(): part = jnp.dot(inputs, block, preferred_element_type=jnp.float32)  21.4 us
    ppermute x12, starting transfers between devices, gather_pieces(): lax.ppermute(ring[-1], 'plane', [(dev, (dev + 1) % 4) for dev in range(4)])  17.2 us
  transfers between devices with their start and end apart: 30, of which 9 were waited for; matrix products, arithmetic and copies ran while one was open for 24% of the time, Pallas kernels for 0%

profile of v1, /device:TPU:8, one launch (start us, length us, event | category | flops | bytes accessed | tf_op | source)
XLA Modules:
  0.0 396.0 jit_solution(7779436592615785248)
XLA Ops:
  7.2 1.4 copy-done
  8.6 1.6 collective-permute-start
  10.2 9.3 %collective-permute-done = bf16[256,768]{1,0:T(8,128)(2,1)S(1)} collective-permute-done((bf16[256,768]{1,0:T(8,128)(2,1)S(1)}, bf16[256,768]{1,0:T(8,128)(2,1)S(1)}, u32[]{:S(2)}, u32[]{:S(2)}) %collective-permute-start) | collective-permute-done | bytes 393248 | tf_op jit(solution)/shard_map/ppermute | solution.py:47
  19.5 1.6 collective-permute-start.1
  21.1 9.3 %collective-permute-done.1 = bf16[256,768]{1,0:T(8,128)(2,1)S(1)} collective-permute-done((bf16[256,768]{1,0:T(8,128)(2,1)S(1)}, bf16[256,768]{1,0:T(8,128)(2,1)S(1)}, u32[]{:S(2)}, u32[]{:S(2)}) %collective-permute-start.1) | collective-permute-done | bytes 393248 | tf_op jit(solution)/shard_map/ppermute | solution.py:47
  32.0 1.6 collective-permute-start.8
  33.6 9.4 %collective-permute-done.2 = bf16[256,768]{1,0:T(8,128)(2,1)} collective-permute-done((bf16[256,768]{1,0:T(8,128)(2,1)S(1)}, bf16[256,768]{1,0:T(8,128)(2,1)}, u32[]{:S(2)}, u32[]{:S(2)}) %collective-permute-start.2) | collective-permute-done | bytes 393248 | tf_op jit(solution)/shard_map/ppermute | solution.py:47
  43.1 10.2 %fusion.28 = bf16[1024,768]{1,0:T(8,128)(2,1)S(1)} fusion(s32[]{:T(128)S(6)} %select_n.105, bf16[256,768]{1,0:T(8,128)(2,1)} %collective-permute-done.2, bf16[256,768]{1,0:T(8,128)(2,1)S(1)} %collective-permute-done.1, bf16[256,768]{1,0:T(8,128)(2,1)S(1)} %collective-permute-done, bf16[256,768]{1,0:T(8,128)(2,1)S(1)} %constant_dynamic-slice_fusion.3), kind=kLoop, calls=%fused_computation.54 | loop fusion | flops 12582912 | bytes 3145732 | tf_op jit(solution)/shard_map/jit(_roll_dynamic)/concatenate | solution.py:48
  53.3 1.1 collective-permute-start.3
  54.4 1.0 constant_dynamic-slice_fusion.1
  55.9 9.8 %collective-permute-done.14 = bf16[256,768]{1,0:T(8,128)(2,1)S(1)} collective-permute-done((bf16[256,768]{1,0:T(8,128)(2,1)S(1)}, bf16[256,768]{1,0:T(8,128)(2,1)S(1)}, u32[]{:S(2)}, u32[]{:S(2)}) %collective-permute-start.14) | collective-permute-done | bytes 393248 | tf_op jit(solution)/shard_map/ppermute | solution.py:47
  65.8 2.7 collective-permute-start.9
  68.6 10.0 %collective-permute-done.9 = bf16[256,256]{1,0:T(8,128)(2,1)} collective-permute-done((bf16[256,256]{1,0:T(8,128)(2,1)}, bf16[256,256]{1,0:T(8,128)(2,1)}, u32[]{:S(2)}, u32[]{:S(2)}) %collective-permute-start.9) | collective-permute-done | bytes 131104 | tf_op jit(solution)/shard_map/ppermute | solution.py:47
  78.7 3.2 collective-permute-start.16
  82.4 3.7 collective-permute-done.3
  86.8 4.3 %fusion.50 = bf16[1024,256]{1,0:T(8,128)(2,1)} fusion(s32[]{:T(128)S(6)} %select_n.105, bf16[256,256]{1,0:T(8,128)(2,1)} %collective-permute-done.10, bf16[256,256]{1,0:T(8,128)(2,1)} %collective-permute-done.9, bf16[256,256]{1,0:T(8,128)(2,1)} %collective-permute-done.8, bf16[256,256]{1,0:T(8,128)(2,1)S(1)} %constant_dynamic-slice_fusion.2), kind=kLoop, calls=%fused_computation.118 | loop fusion | flops 4194304 | bytes 1048580 | tf_op jit(solution)/shard_map/jit(_roll_dynamic)/concatenate | solution.py:48
  91.8 9.8 %fusion.21 = bf16[1024,768]{1,0:T(8,128)(2,1)} fusion(s32[]{:T(128)S(6)} %select_n.105, bf16[256,768]{1,0:T(8,128)(2,1)} %collective-permute-done.16, bf16[256,768]{1,0:T(8,128)(2,1)} %collective-permute-done.15, bf16[256,768]{1,0:T(8,128)(2,1)S(1)} %collective-permute-done.14, bf16[256,768]{1,0:T(8,128)(2,1)S(1)} %constant_dynamic-slice_fusion.1), kind=kLoop, calls=%fused_computation.47 | loop fusion | flops 12582912 | bytes 3145732 | tf_op jit(solution)/shard_map/jit(_roll_dynamic)/concatenate | solution.py:48
  101.6 1.2 collective-permute-start.17
  103.6 2.0 convolution_dynamic-update-slice_fusion.6
  105.6 2.0 convolution_dynamic-update-slice_fusion.5
  109.1 2.7 collective-permute-start.6
  111.8 1.5 collective-permute-start.7
  113.4 1.2 collective-permute-start.12
  114.8 1.3 copy.52
  116.4 23.0 %collective-permute-done.17 = bf16[1024,768]{1,0:T(8,128)(2,1)} collective-permute-done((bf16[1024,768]{1,0:T(8,128)(2,1)}, bf16[1024,768]{1,0:T(8,128)(2,1)}, u32[]{:S(2)}, u32[]{:S(2)}) %collective-permute-start.17) | collective-permute-done | bytes 1572896 | tf_op jit(solution)/shard_map/ppermute | solution.py:57
  139.9 2.4 pad_maximum_fusion.2
  142.4 2.3 copy.53
  144.7 1.4 copy.51
  146.1 2.0 pad_maximum_fusion
  148.1 1.0 fusion.32
  149.1 3.2 fusion.84
  152.4 1.8 fusion.34
  154.9 1.4 convolution_dynamic-update-slice_fusion.15
  156.3 1.4 convolution_dynamic-update-slice_fusion.14
  157.7 1.4 convolution_dynamic-update-slice_fusion.13
  159.1 1.4 convolution_dynamic-update-slice_fusion.12
  160.9 2.0 convolution_dynamic-update-slice_fusion.3
  163.0 2.0 convolution_dynamic-update-slice_fusion.2
  165.0 2.0 convolution_dynamic-update-slice_fusion.1
  167.1 2.0 convolution_dynamic-update-slice_fusion
  170.3 1.6 copy.60
  171.9 6.9 %all-to-all-start.1 = ((bf16[4,8,128,192]{2,3,1,0:T(8,128)(2,1)}), bf16[4,8,128,192]{2,3,1,0:T(8,128)(2,1)S(1)}, u32[]{:S(2)}, u32[]{:S(2)}) async-start(bf16[4,8,128,192]{2,3,1,0:T(8,128)(2,1)} %bitcast.26), calls=%async_computation.1 | async-start | bytes 3145728 | tf_op jit(solution)/shard_map/all_to_all | solution.py:175
  179.7 1.5 collective-permute-start.20
  181.2 34.4 %collective-permute-done.20 = bf16[256,256]{1,0:T(8,128)(2,1)S(1)} collective-permute-done((bf16[256,256]{1,0:T(8,128)(2,1)S(1)}, bf16[256,256]{1,0:T(8,128)(2,1)S(1)}, u32[]{:S(2)}, u32[]{:S(2)}) %collective-permute-start.20) | collective-permute-done | bytes 131104 | tf_op jit(solution)/shard_map/ppermute | solution.py:47
  215.6 2.5 collective-permute-start.21
  218.7 6.9 %all-to-all-start = ((bf16[4,8,128]{2,1,0:T(8,128)(2,1)}), bf16[4,8,128]{2,1,0:T(8,128)(2,1)S(1)}, u32[]{:S(2)}, u32[]{:S(2)}) async-start(bf16[4,8,128]{2,1,0:T(8,128)(2,1)} %broadcast_in_dim.86), calls=%async_computation | async-start | bytes 16384 | tf_op jit(solution)/shard_map/all_to_all | solution.py:176
  225.7 1.7 collective-permute-start.22
  227.3 2.6 copy.68
  229.9 16.5 %while.11 = (s32[]{:T(128)}, bf16[8,512,64]{1,2,0:T(8,128)(2,1)S(1)}, bf16[8,512]{1,0:T(8,128)(2,1)S(1)}, bf16[8,512,192]{2,1,0:T(8,128)(2,1)}, s32[]{:T(128)}) while((s32[]{:T(128)}, bf16[8,512,64]{1,2,0:T(8,128)(2,1)S(1)}, bf16[8,512]{1,0:T(8,128)(2,1)S(1)}, bf16[8,512,192]{2,1,0:T(8,128)(2,1)}, s32[]{:T(128)}) %tuple.50), condition=%wide.region_7.10_spmd.clone, body=%wide.region_4.9_spmd.clone.sunk | while | flops 71336448 | bytes 3945545 | solution.py:105
  229.9 1.0 dynamic-slice_bitcast_fusion.2
  232.0 1.0 dynamic-slice_bitcast_fusion.2
  234.0 1.0 dynamic-slice_bitcast_fusion.2
  236.1 1.0 dynamic-slice_bitcast_fusion.2
  238.1 1.0 dynamic-slice_bitcast_fusion.2
  240.2 1.0 dynamic-slice_bitcast_fusion.2
  242.2 1.0 dynamic-slice_bitcast_fusion.2
  244.3 1.0 dynamic-slice_bitcast_fusion.2
  247.2 1.6 reshape.161
  248.8 4.8 %all-to-all-start.2 = ((bf16[4,2,32768]{2,1,0:T(2,128)(2,1)}), bf16[4,2,32768]{2,1,0:T(2,128)(2,1)S(1)}, u32[]{:S(2)}, u32[]{:S(2)}) async-start(bf16[4,2,32768]{2,1,0:T(2,128)(2,1)} %reshape.161), calls=%async_computation.2 | async-start | bytes 1048576 | tf_op jit(solution)/shard_map/all_to_all | solution.py:179
  253.6 4.8 %fusion.43 = bf16[1024,256]{1,0:T(8,128)(2,1)S(1)} fusion(s32[]{:T(128)S(6)} %select_n.105, bf16[256,256]{1,0:T(8,128)(2,1)S(1)} %collective-permute-done.22, bf16[256,256]{1,0:T(8,128)(2,1)S(1)} %collective-permute-done.21, bf16[256,256]{1,0:T(8,128)(2,1)S(1)} %collective-permute-done.20, bf16[256,256]{1,0:T(8,128)(2,1)S(1)} %constant_dynamic-slice_fusion), kind=kLoop, calls=%fused_computation.111 | loop fusion | flops 4194304 | bytes 1048580 | tf_op jit(solution)/shard_map/jit(_roll_dynamic)/concatenate | solution.py:48
  260.6 30.6 %all-reduce.1 = f32[32]{0:T(128)S(1)} all-reduce(f32[32]{0:T(128)S(1)} %convert_reduce_fusion), channel_id=3, replica_groups=mesh['groups'=2,'sec'=4,'plane'=4] {'sec','plane'}, use_global_device_ids=true, to_apply=%region_10.13.clone | all-reduce | flops 32 | bytes 256
  294.8 1.5 convolution_dynamic-update-slice_fusion.8
  297.4 90.1 %all-reduce.4.cloned.1.call-done = f32[32,1024]{1,0:T(8,128)} async-done(((f32[32,1024]{1,0:T(8,128)}), f32[32,1024]{1,0:T(8,128)}) %all-reduce.4.cloned.1.call-update) | async-done | bytes 131088
  387.5 1.4 dynamic-slice_divide_fusion
  (139 shorter events, 26.8 us)
Async XLA Ops:
  7.2 1.4 copy-start
  8.6 10.9 %collective-permute-start = (bf16[256,768]{1,0:T(8,128)(2,1)S(1)}, bf16[256,768]{1,0:T(8,128)(2,1)S(1)}, u32[]{:S(2)}, u32[]{:S(2)}) collective-permute-start(bf16[256,768]{1,0:T(8,128)(2,1)S(1)} %constant_dynamic-slice_fusion.3), channel_id=1, source_target_pairs={{0,1},{1,2},{2,3},{3,0},{4,5},{5,6},{6,7},{7,4},{8,9},{9,10},{10,1... | collective-permute-start | bytes 1179656 | tf_op jit(solution)/shard_map/ppermute | solution.py:47
  19.5 10.9 %collective-permute-start.1 = (bf16[256,768]{1,0:T(8,128)(2,1)S(1)}, bf16[256,768]{1,0:T(8,128)(2,1)S(1)}, u32[]{:S(2)}, u32[]{:S(2)}) collective-permute-start(bf16[256,768]{1,0:T(8,128)(2,1)S(1)} %collective-permute-done), channel_id=1, source_target_pairs={{0,1},{1,2},{2,3},{3,0},{4,5},{5,6},{6,7},{7,4},{8,9},{9,10},{10,1... | collective-permute-start | bytes 1179656 | tf_op jit(solution)/shard_map/ppermute | solution.py:47
  30.4 12.7 %collective-permute-start.2 = (bf16[256,768]{1,0:T(8,128)(2,1)S(1)}, bf16[256,768]{1,0:T(8,128)(2,1)}, u32[]{:S(2)}, u32[]{:S(2)}) collective-permute-start(bf16[256,768]{1,0:T(8,128)(2,1)S(1)} %collective-permute-done.1), channel_id=1, source_target_pairs={{0,1},{1,2},{2,3},{3,0},{4,5},{5,6},{6,7},{7,4},{8,9},{9,10},{10,1... | collective-permute-start | bytes 1179656 | tf_op jit(solution)/shard_map/ppermute | solution.py:47
  32.0 33.8 %collective-permute-start.8 = (bf16[256,256]{1,0:T(8,128)(2,1)S(1)}, bf16[256,256]{1,0:T(8,128)(2,1)}, u32[]{:S(2)}, u32[]{:S(2)}) collective-permute-start(bf16[256,256]{1,0:T(8,128)(2,1)S(1)} %constant_dynamic-slice_fusion.2), channel_id=1, source_target_pairs={{0,1},{1,2},{2,3},{3,0},{4,5},{5,6},{6,7},{7,4},{8,9},{9,10},{10,1... | collective-permute-start | bytes 393224 | tf_op jit(solution)/shard_map/ppermute | solution.py:47
  33.6 21.9 %copy-start.2 = (bf16[2,128,1024]{2,1,0:T(8,128)(2,1)S(1)}, bf16[2,128,1024]{2,1,0:T(8,128)(2,1)}, u32[]{:S(2)}) copy-start(bf16[2,128,1024]{2,1,0:T(8,128)(2,1)} %param.14) | copy-start | bytes 1572868
  33.6 22.0 %copy-start.7 = (f32[2,1024]{1,0:T(2,128)S(1)}, f32[2,1024]{1,0:T(2,128)}, u32[]{:S(2)}) copy-start(f32[2,1024]{1,0:T(2,128)} %param.17) | copy-start | bytes 24580
  53.3 12.4 %copy-start.10 = (s32[8]{0:T(128)S(1)}, s32[8]{0:T(128)}, u32[]{:S(2)}) copy-start(s32[8]{0:T(128)} %param.15) | copy-start | bytes 100
  53.3 32.8 %collective-permute-start.3 = (bf16[1024,768]{1,0:T(8,128)(2,1)S(1)}, bf16[1024,768]{1,0:T(8,128)(2,1)}, u32[]{:S(2)}, u32[]{:S(2)}) collective-permute-start(bf16[1024,768]{1,0:T(8,128)(2,1)S(1)} %fusion.28), channel_id=1, source_target_pairs={{0,16},{16,0},{1,17},{17,1},{2,18},{18,2},{3,19},{19,3},{4,20},{20... | collective-permute-start | bytes 4718600 | tf_op jit(solution)/shard_map/ppermute | solution.py:57
  55.4 10.3 %collective-permute-start.14 = (bf16[256,768]{1,0:T(8,128)(2,1)S(1)}, bf16[256,768]{1,0:T(8,128)(2,1)S(1)}, u32[]{:S(2)}, u32[]{:S(2)}) collective-permute-start(bf16[256,768]{1,0:T(8,128)(2,1)S(1)} %constant_dynamic-slice_fusion.1), channel_id=1, source_target_pairs={{0,1},{1,2},{2,3},{3,0},{4,5},{5,6},{6,7},{7,4},{8,9},{9,10},{10,1... | collective-permute-start | bytes 1179656 | tf_op jit(solution)/shard_map/ppermute | solution.py:47
  65.7 13.0 %collective-permute-start.15 = (bf16[256,768]{1,0:T(8,128)(2,1)S(1)}, bf16[256,768]{1,0:T(8,128)(2,1)}, u32[]{:S(2)}, u32[]{:S(2)}) collective-permute-start(bf16[256,768]{1,0:T(8,128)(2,1)S(1)} %collective-permute-done.14), channel_id=1, source_target_pairs={{0,1},{1,2},{2,3},{3,0},{4,5},{5,6},{6,7},{7,4},{8,9},{9,10},{10,1... | collective-permute-start | bytes 1179656 | tf_op jit(solution)/shard_map/ppermute | solution.py:47
  65.8 12.9 %collective-permute-start.9 = (bf16[256,256]{1,0:T(8,128)(2,1)}, bf16[256,256]{1,0:T(8,128)(2,1)}, u32[]{:S(2)}, u32[]{:S(2)}) collective-permute-start(bf16[256,256]{1,0:T(8,128)(2,1)} %collective-permute-done.8), channel_id=1, source_target_pairs={{0,1},{1,2},{2,3},{3,0},{4,5},{5,6},{6,7},{7,4},{8,9},{9,10},{10,1... | collective-permute-start | bytes 393224 | tf_op jit(solution)/shard_map/ppermute | solution.py:47
  68.6 37.0 %collective-permute-start.4 = (bf16[1024,768]{1,0:T(8,128)(2,1)S(1)}, bf16[1024,768]{1,0:T(8,128)(2,1)}, u32[]{:S(2)}, u32[]{:S(2)}) collective-permute-start(bf16[1024,768]{1,0:T(8,128)(2,1)S(1)} %fusion.28), channel_id=1, source_target_pairs={{0,4},{4,0},{8,12},{12,8},{1,5},{5,1},{9,13},{13,9},{2,6},{6,2},{1... | collective-permute-start | bytes 4718600 | tf_op jit(solution)/shard_map/ppermute | solution.py:62
  78.7 8.1 %collective-permute-start.10 = (bf16[256,256]{1,0:T(8,128)(2,1)}, bf16[256,256]{1,0:T(8,128)(2,1)}, u32[]{:S(2)}, u32[]{:S(2)}) collective-permute-start(bf16[256,256]{1,0:T(8,128)(2,1)} %collective-permute-done.9), channel_id=1, source_target_pairs={{0,1},{1,2},{2,3},{3,0},{4,5},{5,6},{6,7},{7,4},{8,9},{9,10},{10,1... | collective-permute-start | bytes 393224 | tf_op jit(solution)/shard_map/ppermute | solution.py:47
  78.7 13.2 %collective-permute-start.16 = (bf16[256,768]{1,0:T(8,128)(2,1)}, bf16[256,768]{1,0:T(8,128)(2,1)}, u32[]{:S(2)}, u32[]{:S(2)}) collective-permute-start(bf16[256,768]{1,0:T(8,128)(2,1)} %collective-permute-done.15), channel_id=1, source_target_pairs={{0,1},{1,2},{2,3},{3,0},{4,5},{5,6},{6,7},{7,4},{8,9},{9,10},{10,1... | collective-permute-start | bytes 1179656 | tf_op jit(solution)/shard_map/ppermute | solution.py:47
  86.1 21.5 %collective-permute-start.5 = (bf16[1024,768]{1,0:T(8,128)(2,1)}, bf16[1024,768]{1,0:T(8,128)(2,1)S(1)}, u32[]{:S(2)}, u32[]{:S(2)}) collective-permute-start(bf16[1024,768]{1,0:T(8,128)(2,1)} %collective-permute-done.3), channel_id=1, source_target_pairs={{0,4},{4,0},{8,12},{12,8},{1,5},{5,1},{9,13},{13,9},{2,6},{6,2},{1... | collective-permute-start | bytes 4718600 | tf_op jit(solution)/shard_map/ppermute | solution.py:62
  91.1 23.6 %collective-permute-start.11 = (bf16[1024,256]{1,0:T(8,128)(2,1)}, bf16[1024,256]{1,0:T(8,128)(2,1)}, u32[]{:S(2)}, u32[]{:S(2)}) collective-permute-start(bf16[1024,256]{1,0:T(8,128)(2,1)} %fusion.50), channel_id=1, source_target_pairs={{0,16},{16,0},{1,17},{17,1},{2,18},{18,2},{3,19},{19,3},{4,20},{20... | collective-permute-start | bytes 1572872 | tf_op jit(solution)/shard_map/ppermute | solution.py:57
  101.6 37.8 %collective-permute-start.17 = (bf16[1024,768]{1,0:T(8,128)(2,1)}, bf16[1024,768]{1,0:T(8,128)(2,1)}, u32[]{:S(2)}, u32[]{:S(2)}) collective-permute-start(bf16[1024,768]{1,0:T(8,128)(2,1)} %fusion.21), channel_id=1, source_target_pairs={{0,16},{16,0},{1,17},{17,1},{2,18},{18,2},{3,19},{19,3},{4,20},{20... | collective-permute-start | bytes 4718600 | tf_op jit(solution)/shard_map/ppermute | solution.py:57
  109.1 30.3 %collective-permute-start.6 = (bf16[128,2048]{1,0:T(8,128)(2,1)}, bf16[128,2048]{1,0:T(8,128)(2,1)}, u32[]{:S(2)}, u32[]{:S(2)}) collective-permute-start(bf16[128,2048]{1,0:T(8,128)(2,1)} %get-tuple-element.87), channel_id=1, source_target_pairs={{0,4},{4,8},{8,12},{1,5},{5,9},{9,13},{2,6},{6,10},{10,14},{3,7},{... | collective-permute-start | bytes 1572872 | tf_op jit(solution)/shard_map/ppermute | solution.py:16
  111.8 28.1 %collective-permute-start.7 = (bf16[128,2048]{1,0:T(8,128)(2,1)S(1)}, bf16[128,2048]{1,0:T(8,128)(2,1)}, u32[]{:S(2)}, u32[]{:S(2)}) collective-permute-start(bf16[128,2048]{1,0:T(8,128)(2,1)S(1)} %get-tuple-element.88), channel_id=1, source_target_pairs={{4,0},{8,4},{12,8},{5,1},{9,5},{13,9},{6,2},{10,6},{14,10},{7,3},{... | collective-permute-start | bytes 1572872 | tf_op jit(solution)/shard_map/ppermute | solution.py:16
  113.4 44.3 %collective-permute-start.12 = (bf16[1024,256]{1,0:T(8,128)(2,1)}, bf16[1024,256]{1,0:T(8,128)(2,1)}, u32[]{:S(2)}, u32[]{:S(2)}) collective-permute-start(bf16[1024,256]{1,0:T(8,128)(2,1)} %fusion.50), channel_id=1, source_target_pairs={{0,4},{4,0},{8,12},{12,8},{1,5},{5,1},{9,13},{13,9},{2,6},{6,2},{1... | collective-permute-start | bytes 1572872 | tf_op jit(solution)/shard_map/ppermute | solution.py:62
  114.6 44.5 %collective-permute-start.13 = (bf16[1024,256]{1,0:T(8,128)(2,1)}, bf16[1024,256]{1,0:T(8,128)(2,1)}, u32[]{:S(2)}, u32[]{:S(2)}) collective-permute-start(bf16[1024,256]{1,0:T(8,128)(2,1)} %collective-permute-done.11), channel_id=1, source_target_pairs={{0,4},{4,0},{8,12},{12,8},{1,5},{5,1},{9,13},{13,9},{2,6},{6,2},{1... | collective-permute-start | bytes 1572872 | tf_op jit(solution)/shard_map/ppermute | solution.py:62
  139.4 25.6 %collective-permute-start.18 = (bf16[1024,768]{1,0:T(8,128)(2,1)}, bf16[1024,768]{1,0:T(8,128)(2,1)}, u32[]{:S(2)}, u32[]{:S(2)}) collective-permute-start(bf16[1024,768]{1,0:T(8,128)(2,1)} %fusion.21), channel_id=1, source_target_pairs={{0,4},{4,0},{8,12},{12,8},{1,5},{5,1},{9,13},{13,9},{2,6},{6,2},{1... | collective-permute-start | bytes 4718600 | tf_op jit(solution)/shard_map/ppermute | solution.py:62
  139.4 27.7 %collective-permute-start.19 = (bf16[1024,768]{1,0:T(8,128)(2,1)}, bf16[1024,768]{1,0:T(8,128)(2,1)}, u32[]{:S(2)}, u32[]{:S(2)}) collective-permute-start(bf16[1024,768]{1,0:T(8,128)(2,1)} %collective-permute-done.17), channel_id=1, source_target_pairs={{0,4},{4,0},{8,12},{12,8},{1,5},{5,1},{9,13},{13,9},{2,6},{6,2},{1... | collective-permute-start | bytes 4718600 | tf_op jit(solution)/shard_map/ppermute | solution.py:62
  144.7 1.4 copy-start.3
  160.7 6.4 %copy-start.5 = (bf16[256,1024]{1,0:T(8,128)(2,1)}, bf16[256,1024]{1,0:T(8,128)(2,1)S(1)}, u32[]{:S(2)}) copy-start(bf16[256,1024]{1,0:T(8,128)(2,1)S(1)} %get-tuple-element.84) | copy-start | bytes 1572868
  171.9 46.2 %copy-start.9 = (bf16[2,128]{1,0:T(2,128)(2,1)S(1)}, bf16[2,128]{1,0:T(2,128)(2,1)}, u32[]{:S(2)}) copy-start(bf16[2,128]{1,0:T(2,128)(2,1)} %get-tuple-element.94) | copy-start | bytes 1540
  171.9 46.2 %all-to-all-start.1 = ((bf16[4,8,128,192]{2,3,1,0:T(8,128)(2,1)}), bf16[4,8,128,192]{2,3,1,0:T(8,128)(2,1)S(1)}, u32[]{:S(2)}, u32[]{:S(2)}) async-start(bf16[4,8,128,192]{2,3,1,0:T(8,128)(2,1)} %bitcast.26), calls=%async_computation.1 | async-start | bytes 3145728 | tf_op jit(solution)/shard_map/all_to_all | solution.py:175
  179.7 35.9 %collective-permute-start.20 = (bf16[256,256]{1,0:T(8,128)(2,1)S(1)}, bf16[256,256]{1,0:T(8,128)(2,1)S(1)}, u32[]{:S(2)}, u32[]{:S(2)}) collective-permute-start(bf16[256,256]{1,0:T(8,128)(2,1)S(1)} %constant_dynamic-slice_fusion), channel_id=1, source_target_pairs={{0,1},{1,2},{2,3},{3,0},{4,5},{5,6},{6,7},{7,4},{8,9},{9,10},{10,1... | collective-permute-start | bytes 393224 | tf_op jit(solution)/shard_map/ppermute | solution.py:47
  215.6 10.0 %collective-permute-start.21 = (bf16[256,256]{1,0:T(8,128)(2,1)S(1)}, bf16[256,256]{1,0:T(8,128)(2,1)S(1)}, u32[]{:S(2)}, u32[]{:S(2)}) collective-permute-start(bf16[256,256]{1,0:T(8,128)(2,1)S(1)} %collective-permute-done.20), channel_id=1, source_target_pairs={{0,1},{1,2},{2,3},{3,0},{4,5},{5,6},{6,7},{7,4},{8,9},{9,10},{10,1... | collective-permute-start | bytes 393224 | tf_op jit(solution)/shard_map/ppermute | solution.py:47
  218.7 11.1 %all-to-all-start = ((bf16[4,8,128]{2,1,0:T(8,128)(2,1)}), bf16[4,8,128]{2,1,0:T(8,128)(2,1)S(1)}, u32[]{:S(2)}, u32[]{:S(2)}) async-start(bf16[4,8,128]{2,1,0:T(8,128)(2,1)} %broadcast_in_dim.86), calls=%async_computation | async-start | bytes 16384 | tf_op jit(solution)/shard_map/all_to_all | solution.py:176
  225.7 27.9 %collective-permute-start.22 = (bf16[256,256]{1,0:T(8,128)(2,1)S(1)}, bf16[256,256]{1,0:T(8,128)(2,1)S(1)}, u32[]{:S(2)}, u32[]{:S(2)}) collective-permute-start(bf16[256,256]{1,0:T(8,128)(2,1)S(1)} %collective-permute-done.21), channel_id=1, source_target_pairs={{0,1},{1,2},{2,3},{3,0},{4,5},{5,6},{6,7},{7,4},{8,9},{9,10},{10,1... | collective-permute-start | bytes 393224 | tf_op jit(solution)/shard_map/ppermute | solution.py:47
  247.2 12.0 %copy-start.8 = (s32[2,128]{1,0:T(2,128)S(1)}, s32[2,128]{1,0:T(2,128)}, u32[]{:S(2)}) copy-start(s32[2,128]{1,0:T(2,128)} %param.16) | copy-start | bytes 3076
  247.2 12.1 %copy-start.11 = (u32[32]{0:T(128)S(1)}, u32[32]{0:T(128)}, u32[]{:S(2)}) copy-start(u32[32]{0:T(128)} %constant.149) | copy-start | bytes 388
  248.8 42.5 %all-to-all-start.2 = ((bf16[4,2,32768]{2,1,0:T(2,128)(2,1)}), bf16[4,2,32768]{2,1,0:T(2,128)(2,1)S(1)}, u32[]{:S(2)}, u32[]{:S(2)}) async-start(bf16[4,2,32768]{2,1,0:T(2,128)(2,1)} %reshape.161), calls=%async_computation.2 | async-start | bytes 1048576 | tf_op jit(solution)/shard_map/all_to_all | solution.py:179
  253.6 133.9 %all-reduce.4.cloned.1.call-start = ((), (), s32[]{:S(2)}) async-start(), calls=%async_computation.3 | async-start | bytes 262144
  258.4 32.8 %collective-permute-start.23 = (bf16[1024,256]{1,0:T(8,128)(2,1)S(1)}, bf16[1024,256]{1,0:T(8,128)(2,1)S(1)}, u32[]{:S(2)}, u32[]{:S(2)}) collective-permute-start(bf16[1024,256]{1,0:T(8,128)(2,1)S(1)} %fusion.43), channel_id=1, source_target_pairs={{0,16},{16,0},{1,17},{17,1},{2,18},{18,2},{3,19},{19,3},{4,20},{20... | collective-permute-start | bytes 1572872 | tf_op jit(solution)/shard_map/ppermute | solution.py:57
  259.2 35.2 %collective-permute-start.24 = (bf16[1024,256]{1,0:T(8,128)(2,1)S(1)}, bf16[1024,256]{1,0:T(8,128)(2,1)S(1)}, u32[]{:S(2)}, u32[]{:S(2)}) collective-permute-start(bf16[1024,256]{1,0:T(8,128)(2,1)S(1)} %fusion.43), channel_id=1, source_target_pairs={{0,4},{4,0},{8,12},{12,8},{1,5},{5,1},{9,13},{13,9},{2,6},{6,2},{1... | collective-permute-start | bytes 1572872 | tf_op jit(solution)/shard_map/ppermute | solution.py:62
  291.2 3.5 collective-permute-start.25
  294.3 1.9 copy-start.6
  294.7 94.2 %copy-start.1 = (bf16[256,3072]{1,0:T(8,128)(2,1)S(1)}, bf16[256,3072]{1,0:T(8,128)(2,1)}, u32[]{:S(2)}) copy-start(bf16[256,3072]{1,0:T(8,128)(2,1)} %param.18) | copy-start | bytes 4718596
  296.4 92.5 %copy-start.4 = (bf16[256,1024]{1,0:T(8,128)(2,1)}, bf16[256,1024]{1,0:T(8,128)(2,1)S(1)}, u32[]{:S(2)}) copy-start(bf16[256,1024]{1,0:T(8,128)(2,1)S(1)} %fusion.38) | copy-start | bytes 1572868
Sparse Core Ops, SparseCore 0:
  297.4 90.0 all-reduce.3
